TPU v7x, 128 devices: a whole 4x4x4 slice. The times are simulated.
128 devices in a mesh: kz: 4 (over x_hi, core), en: 32 (over z, y, x_lo).
Axes of the slice: x: 4 (x_hi: 2, x_lo: 2; x = x_hi * 2 + x_lo), y: 4, z: 4, core: 2. Of those that a mesh axis runs over, the one named last changes fastest.
Arguments:
- sigma_less: bfloat16 [4, 128, 3, 2, 128, 128], P('kz', 'en'), as said below
- sigma_great: bfloat16 [4, 128, 3, 2, 128, 128], P('kz', 'en'), as said below
- onsite_table: float32 [3, 128, 128], replicated, as said below
- cos_coupling: float32 [3, 128, 128], replicated, as said below
- slab_coupling: float32 [2, 128, 128], replicated, may hold values from -0.25 to 0.25
- slab_kind: int32 [3], replicated, may hold values from 0 to 2, as said below
- kz_table: int32 [4, 4], replicated, may hold values from 0 to 3, as said below
- mode_weight: float32 [2, 4], replicated, may hold values from 0.25 to 2
- form_factor: float32 [2, 128, 128], replicated, as said below
- occupation: float32 [2], replicated, may hold values from 0.1 to 2
- energy_offset: int32 [2], replicated, may hold values from 1 to 4, as said below
Outputs:
- sigma_less_new: bfloat16 [4, 128, 3, 2, 128, 128], P('kz', 'en')
- sigma_great_new: bfloat16 [4, 128, 3, 2, 128, 128], P('kz', 'en')
Inputs may be any that keep to these rules, and one draw needn't show every extreme that they name: `sigma_less`: each block is i times a Hermitian matrix. `sigma_great`: each block is -i times a Hermitian matrix. `onsite_table`: each block is symmetric. `cos_coupling`: each block is symmetric. `form_factor`: each block is symmetric and positive. `kz_table`: each row names every momentum once. `slab_kind`: every kind is used by some slab. `energy_offset`: the modes have different offsets, and some mode has exactly 4.
All inputs are finite; a program needn't handle non-finite values.
Results may differ from a plain program's by a relative error of at most 0.0029.
Values may be sent and summed in bfloat16 or wider, within the bound.
No kernel may reach another device: no remote copies, remote signals or barrier semaphores. Data moves between devices by JAX's collectives and lax.ppermute only.
A program may use at most 128 MiB of HBM per device.

v0:
```python
import jax
import jax.numpy as jnp
from jax import lax
from jax.sharding import PartitionSpec as P

OFFMAX = 4
DAMPING = 0.3


def padded(block, sides, width):
    for axis, dim in sides:
        count = lax.axis_size(axis)
        forward = [(i, i + 1) for i in range(count - 1)]
        backward = [(target, source) for source, target in forward]
        low = lax.ppermute(
            lax.slice_in_dim(block, block.shape[dim] - width, None, axis=dim), axis, forward
        )
        high = lax.ppermute(lax.slice_in_dim(block, 0, width, axis=dim), axis, backward)
        block = jnp.concatenate([low, block, high], axis=dim)
    return block


def matmul_high(left_matrix, right_matrix):
    return jnp.matmul(left_matrix, right_matrix, precision=lax.Precision.HIGHEST)


def complex_product(left_pair, right_pair):
    real_part = matmul_high(left_pair[0], right_pair[0]) - matmul_high(left_pair[1], right_pair[1])
    imag_part = matmul_high(left_pair[0], right_pair[1]) + matmul_high(left_pair[1], right_pair[0])
    return (real_part, imag_part)


def real_left(matrix, pair_value):
    return (matmul_high(matrix, pair_value[0]), matmul_high(matrix, pair_value[1]))


def real_right(pair_value, matrix):
    return (matmul_high(pair_value[0], matrix), matmul_high(pair_value[1], matrix))


def adjoint(pair_value):
    return (jnp.swapaxes(pair_value[0], -1, -2), -jnp.swapaxes(pair_value[1], -1, -2))


def add_pair(left_pair, right_pair):
    return (left_pair[0] + right_pair[0], left_pair[1] + right_pair[1])


def sub_pair(left_pair, right_pair):
    return (left_pair[0] - right_pair[0], left_pair[1] - right_pair[1])


def invert_pair(pair_value):
    orbitals = pair_value[0].shape[-1]
    upper_half = jnp.concatenate([pair_value[0], -pair_value[1]], axis=-1)
    lower_half = jnp.concatenate([pair_value[1], pair_value[0]], axis=-1)
    embedded = jnp.concatenate([upper_half, lower_half], axis=-2)
    transposed = jnp.swapaxes(embedded, -1, -2)
    normal = matmul_high(transposed, embedded)
    factor = jnp.linalg.cholesky(normal)
    solved = jax.scipy.linalg.cho_solve((factor, True), transposed)
    return (solved[..., :orbitals, :orbitals], solved[..., orbitals:, :orbitals])


def greater_of(less_pair, ret_pair):
    return sub_pair(add_pair(less_pair, ret_pair), adjoint(ret_pair))


def pack_pair(pair_value):
    return jnp.stack([pair_value[0], pair_value[1]], axis=-3)


def green_blocks(sigma_less, sigma_great, hamilton, slab_coupling, energies):
    orbitals = sigma_less.shape[-1]
    slab_count = sigma_less.shape[2]
    identity = jnp.eye(orbitals, dtype=jnp.float32)
    energy_grid = energies[None, :, None, None]
    left_ret = []
    left_less = []
    for slab_index in range(slab_count):
        lesser = sigma_less[:, :, slab_index].astype(jnp.float32)
        greater = sigma_great[:, :, slab_index].astype(jnp.float32)
        retarded_re = 0.5 * (greater[:, :, 0] - lesser[:, :, 0])
        retarded_im = 0.5 * (greater[:, :, 1] - lesser[:, :, 1]) - DAMPING * identity
        system_re = energy_grid * identity - hamilton[:, :, slab_index] - retarded_re
        system_im = -retarded_im
        source = (lesser[:, :, 0], lesser[:, :, 1])
        if slab_index > 0:
            coupling = slab_coupling[slab_index - 1]
            folded = real_right(real_left(coupling, left_ret[-1]), coupling.T)
            system_re = system_re - folded[0]
            system_im = system_im - folded[1]
            source = add_pair(source, real_right(real_left(coupling, left_less[-1]), coupling.T))
        inverse = invert_pair((system_re, system_im))
        left_ret.append(inverse)
        left_less.append(complex_product(complex_product(inverse, source), adjoint(inverse)))
    full_ret = left_ret[-1]
    full_less = left_less[-1]
    lesser_list = [full_less]
    greater_list = [greater_of(full_less, full_ret)]
    for slab_index in range(slab_count - 2, -1, -1):
        coupling = slab_coupling[slab_index]
        green_couple = real_right(left_ret[slab_index], coupling)
        bridge = real_right(complex_product(green_couple, full_ret), coupling.T)
        cross_term = complex_product(bridge, left_less[slab_index])
        spread = complex_product(
            real_right(complex_product(green_couple, full_less), coupling.T),
            adjoint(left_ret[slab_index]),
        )
        full_less = add_pair(
            add_pair(left_less[slab_index], spread), sub_pair(cross_term, adjoint(cross_term))
        )
        full_ret = add_pair(left_ret[slab_index], complex_product(bridge, left_ret[slab_index]))
        lesser_list.insert(0, full_less)
        greater_list.insert(0, greater_of(full_less, full_ret))
    lesser_all = jnp.stack([pack_pair(item) for item in lesser_list], axis=2)
    greater_all = jnp.stack([pack_pair(item) for item in greater_list], axis=2)
    return jnp.stack([lesser_all, greater_all], axis=2).astype(jnp.bfloat16)


def hamiltonian(onsite_table, cos_coupling, slab_kind, momenta_index, momenta_total):
    kind_count = onsite_table.shape[0]
    choose = (slab_kind[:, None] == jnp.arange(kind_count, dtype=jnp.int32)[None, :]).astype(
        jnp.float32
    )
    onsite = jnp.einsum("sk,kij->sij", choose, onsite_table, precision=lax.Precision.HIGHEST)
    phase_factor = jnp.cos(2.0 * jnp.pi * momenta_index.astype(jnp.float32) / momenta_total)
    hamilton = onsite[None] + phase_factor[:, None, None, None] * cos_coupling[None]
    return hamilton[:, None]


def momentum_weights(table_rows, mode_weight, momenta_total):
    onehot = (
        table_rows[:, :, None] == jnp.arange(momenta_total, dtype=jnp.int32)[None, None, :]
    ).astype(jnp.float32)
    return (
        jnp.einsum("lq,aqk->lak", mode_weight, onehot, precision=lax.Precision.HIGHEST)
        / momenta_total
    )


def mixed_sums(extended, weights, form_factor, occupation, energy_offset, energy_count, margin):
    total_less = None
    total_great = None
    for mode_index in range(form_factor.shape[0]):
        shift_steps = energy_offset[mode_index]
        upper_side = lax.dynamic_slice_in_dim(extended, margin + shift_steps, energy_count, 1)
        lower_side = lax.dynamic_slice_in_dim(extended, margin - shift_steps, energy_count, 1)
        occupied = occupation[mode_index]
        less_term = (occupied + 1.0) * upper_side[:, :, 0].astype(
            jnp.float32
        ) + occupied * lower_side[:, :, 0].astype(jnp.float32)
        great_term = (occupied + 1.0) * lower_side[:, :, 1].astype(
            jnp.float32
        ) + occupied * upper_side[:, :, 1].astype(jnp.float32)
        less_sum = form_factor[mode_index] * jnp.einsum(
            "ak,kesrij->aesrij", weights[mode_index], less_term, precision=lax.Precision.HIGHEST
        )
        great_sum = form_factor[mode_index] * jnp.einsum(
            "ak,kesrij->aesrij", weights[mode_index], great_term, precision=lax.Precision.HIGHEST
        )
        total_less = less_sum if total_less is None else total_less + less_sum
        total_great = great_sum if total_great is None else total_great + great_sum
    return (total_less, total_great)


def on_device(
    sigma_less,
    sigma_great,
    onsite_table,
    cos_coupling,
    slab_coupling,
    slab_kind,
    kz_table,
    mode_weight,
    form_factor,
    occupation,
    energy_offset,
):
    momenta_local = sigma_less.shape[0]
    energy_local = sigma_less.shape[1]
    momenta_total = momenta_local * lax.axis_size("kz")
    energy_total = energy_local * lax.axis_size("en")
    momenta_start = lax.axis_index("kz") * momenta_local
    momenta_index = momenta_start + jnp.arange(momenta_local, dtype=jnp.int32)
    energy_index = lax.axis_index("en") * energy_local + jnp.arange(energy_local, dtype=jnp.int32)
    energies = -1.5 + 3.0 * (energy_index.astype(jnp.float32) + 0.5) / energy_total
    hamilton = hamiltonian(onsite_table, cos_coupling, slab_kind, momenta_index, momenta_total)
    blocks = green_blocks(sigma_less, sigma_great, hamilton, slab_coupling, energies)
    table_rows = lax.dynamic_slice_in_dim(kz_table, momenta_start, momenta_local, 0)
    weights = momentum_weights(table_rows, mode_weight, momenta_total)
    everyone = lax.all_gather(blocks, "kz", axis=0, tiled=True)
    extended = padded(everyone, (("en", 1),), OFFMAX)
    less_total, great_total = mixed_sums(
        extended, weights, form_factor, occupation, energy_offset, energy_local, OFFMAX
    )
    return (less_total.astype(jnp.bfloat16), great_total.astype(jnp.bfloat16))


def solution(mesh):
    in_specs = (
        P("kz", "en", None, None, None, None),
        P("kz", "en", None, None, None, None),
        P(),
        P(),
        P(),
        P(),
        P(),
        P(),
        P(),
        P(),
        P(),
    )
    out_specs = (P("kz", "en", None, None, None, None), P("kz", "en", None, None, None, None))
    return jax.shard_map(
        on_device, mesh=mesh, in_specs=in_specs, out_specs=out_specs, check_vma=False
    )
```

profile of v0, /device:TPU:1, one launch (start us, length us, event | category | flops | bytes accessed | tf_op | source)
XLA Modules:
  0.0 1280.6 jit_solution(12174855667015090132)
XLA Ops:
  7.4 2.0 fusion.356
  9.4 2.0 fusion.357
  14.7 1.9 fusion.44
  20.6 47.1 %custom-call.23 = f32[1,4,128,128]{3,2,1,0:T(8,128)S(1)} custom-call(f32[1,4,128,128]{3,2,1,0:T(8,128)S(1)} %cholesky.281), custom_call_target="Cholesky" | custom-call | tf_op jit(solution)/shard_map/jit(cholesky)/cholesky | solution.py:60
  67.7 39.3 %custom-call.24 = f32[1,4,1,128,128]{3,4,2,1,0:T(8,128)S(1)} custom-call(f32[1,4,1,128,128]{4,3,2,1,0:T(8,128)S(1)} %select_bitcast_fusion.2), custom_call_target="InvertDiagBlocksLowerTriangular" | custom-call | tf_op jit(solution)/shard_map/jit(cholesky)/cholesky | solution.py:60
  110.1 46.9 %custom-call.25 = f32[1,4,128,128]{3,2,1,0:T(8,128)S(1)} custom-call(f32[1,4,128,128]{3,2,1,0:T(8,128)S(1)} %fusion.25), custom_call_target="Cholesky" | custom-call | tf_op jit(solution)/shard_map/jit(cholesky)/cholesky | solution.py:60
  159.6 4.1 while.6
  163.7 78.8 %custom-call.26 = f32[4,2,128,128]{2,3,1,0:T(8,128)S(1)} custom-call(f32[4,2,128,128]{3,2,1,0:T(8,128)S(1)} %bitcast.917), custom_call_target="InvertDiagBlocksLowerTriangular" | custom-call | tf_op jit(solution)/shard_map/jit(_cho_solve)/vmap()/triangular_solve | solution.py:61
  258.9 47.3 %custom-call.27 = f32[1,4,128,128]{3,2,1,0:T(8,128)S(1)} custom-call(f32[1,4,128,128]{3,2,1,0:T(8,128)S(1)} %cholesky.284), custom_call_target="Cholesky" | custom-call | tf_op jit(solution)/shard_map/jit(cholesky)/cholesky | solution.py:60
  306.4 39.3 %custom-call.28 = f32[1,4,1,128,128]{3,4,2,1,0:T(8,128)S(1)} custom-call(f32[1,4,1,128,128]{4,3,2,1,0:T(8,128)S(1)} %select_bitcast_fusion.1), custom_call_target="InvertDiagBlocksLowerTriangular" | custom-call | tf_op jit(solution)/shard_map/jit(cholesky)/cholesky | solution.py:60
  348.7 46.9 %custom-call.29 = f32[1,4,128,128]{3,2,1,0:T(8,128)S(1)} custom-call(f32[1,4,128,128]{3,2,1,0:T(8,128)S(1)} %fusion.26), custom_call_target="Cholesky" | custom-call | tf_op jit(solution)/shard_map/jit(cholesky)/cholesky | solution.py:60
  396.2 4.1 while.7
  400.2 78.8 %custom-call.30 = f32[4,2,128,128]{2,3,1,0:T(8,128)S(1)} custom-call(f32[4,2,128,128]{3,2,1,0:T(8,128)S(1)} %bitcast.918), custom_call_target="InvertDiagBlocksLowerTriangular" | custom-call | tf_op jit(solution)/shard_map/jit(_cho_solve)/vmap()/triangular_solve | solution.py:61
  479.1 1.9 fusion.53
  497.9 2.1 fusion.40
  510.8 47.3 %custom-call.31 = f32[1,4,128,128]{3,2,1,0:T(8,128)S(1)} custom-call(f32[1,4,128,128]{3,2,1,0:T(8,128)S(1)} %cholesky.287), custom_call_target="Cholesky" | custom-call | tf_op jit(solution)/shard_map/jit(cholesky)/cholesky | solution.py:60
  561.3 40.8 %custom-call.32 = f32[1,4,1,128,128]{3,4,2,1,0:T(8,128)} custom-call(f32[1,4,1,128,128]{4,3,2,1,0:T(8,128)} %select_bitcast_fusion), custom_call_target="InvertDiagBlocksLowerTriangular" | custom-call | tf_op jit(solution)/shard_map/jit(cholesky)/cholesky | solution.py:60
  603.5 2.3 fusion.27
  605.8 48.4 %custom-call.33 = f32[1,4,128,128]{3,2,1,0:T(8,128)} custom-call(f32[1,4,128,128]{3,2,1,0:T(8,128)} %fusion.27), custom_call_target="Cholesky" | custom-call | tf_op jit(solution)/shard_map/jit(cholesky)/cholesky | solution.py:60
  658.6 6.8 while.8
  659.8 2.1 bitcast_dynamic-update-slice_fusion.11
  663.2 2.1 bitcast_dynamic-update-slice_fusion.11
  665.3 80.2 %custom-call.34 = f32[4,2,128,128]{2,3,1,0:T(8,128)} custom-call(f32[4,2,128,128]{3,2,1,0:T(8,128)} %bitcast.916), custom_call_target="InvertDiagBlocksLowerTriangular" | custom-call | tf_op jit(solution)/shard_map/jit(_cho_solve)/vmap()/triangular_solve | solution.py:61
  745.6 1.8 fusion.51
  792.5 2.0 fusion.32
  796.3 2.2 fusion.17
  800.3 2.0 fusion.33
  808.6 2.4 fusion.370
  819.5 2.3 convolution_subtract_fusion.7
  823.6 2.1 fusion.30
  830.1 2.5 fusion.10
  834.4 2.1 fusion.31
  840.0 1.9 convert_bitcast_fusion.2
  847.5 2.1 convert_bitcast_fusion.5
  849.6 2.0 convert_bitcast_fusion.4
  856.0 54.2 %all-gather.2.cloned.1.call-done = bf16[4,4,2,3,2,128,128]{6,5,4,3,2,1,0:T(8,128)(2,1)} async-done(((bf16[1,4,2,3,2,128,128]{6,5,4,3,2,1,0:T(8,128)(2,1)}), bf16[4,4,2,3,2,128,128]{6,5,4,3,2,1,0:T(8,128)(2,1)}) %all-gather.2.cloned.1.call-update) | async-done | bytes 6291472 | tf_op jit(solution)/shard_map/all_gather | solution.py:192
  910.2 4.9 collective-permute-start
  925.1 122.2 %collective-permute-done = bf16[4,4,2,3,2,128,128]{6,5,4,3,2,1,0:T(8,128)(2,1)} collective-permute-done((bf16[4,4,2,3,2,128,128]{6,5,4,3,2,1,0:T(8,128)(2,1)}, bf16[4,4,2,3,2,128,128]{6,5,4,3,2,1,0:T(8,128)(2,1)}, u32[]{:S(2)}, u32[]{:S(2)}) %collective-permute-start) | collective-permute-done | bytes 6291488 | tf_op jit(solution)/shard_map/ppermute | solution.py:15
  1047.3 8.0 constant_dynamic-update-slice_fusion.2
  1055.3 4.1 constant_dynamic-update-slice_fusion.1
  1059.4 125.6 %collective-permute-done.1 = bf16[4,4,2,3,2,128,128]{6,5,4,3,2,1,0:T(8,128)(2,1)} collective-permute-done((bf16[4,4,2,3,2,128,128]{6,5,4,3,2,1,0:T(8,128)(2,1)}, bf16[4,4,2,3,2,128,128]{6,5,4,3,2,1,0:T(8,128)(2,1)}, u32[]{:S(2)}, u32[]{:S(2)}) %collective-permute-start.1) | collective-permute-done | bytes 6291488 | tf_op jit(solution)/shard_map/ppermute | solution.py:18
  1185.0 8.1 constant_dynamic-update-slice_fusion
  1193.0 18.2 %add_bitcast_fusion.1 = (f32[4,4,3,2,128,128]{5,4,3,2,1,0:T(8,128)S(1)}, f32[4,4,3,2,128,128]{5,4,3,2,1,0:T(8,128)}, f32[4,4,3,2,128,128]{5,4,3,2,1,0:T(8,128)}, f32[4,4,3,2,128,128]{5,4,3,2,1,0:T(8,128)}) fusion(bf16[4,12,2,3,2,128,128]{6,5,4,3,2,1,0:T(8,128)(2,1)} %constant_dynamic-update-slice_fusion, s32[]{:T(128)S(6)} %select_n.19, s32[]{:T(128)S(6)} %add.377, ...), kind=kLoop, calls=%fused_computation.15 | loop fusion | flops 31457280 | bytes 50331684 | tf_op jit(solution)/shard_map/add | solution.py:153
  1211.3 19.0 %fusion.6 = f32[1,4,3,2,128,128]{5,0,4,3,2,1:T(1,128)S(1)} fusion(f32[4,4,3,2,128,128]{5,4,3,2,1,0:T(8,128)} %get-tuple-element.68, f32[2,4]{1,0:T(2,128)S(1)} %fusion.36), kind=kOutput, calls=%fused_computation.12 | convolution fusion | flops 18874368 | bytes 7864832 | tf_op jit(solution)/shard_map/ak,kesrij->aesrij/dot_general | solution.py:156
  1230.2 13.8 %fusion.4 = f32[1,4,3,2,128,128]{5,0,4,3,2,1:T(1,128)S(1)} fusion(f32[4,4,3,2,128,128]{5,4,3,2,1,0:T(8,128)S(1)} %copy-done.3, f32[2,4]{1,0:T(2,128)S(1)} %fusion.36), kind=kOutput, calls=%fused_computation.10 | convolution fusion | flops 18874368 | bytes 7864832 | tf_op jit(solution)/shard_map/ak,kesrij->aesrij/dot_general | solution.py:156
  1244.1 13.6 %fusion.2 = f32[1,4,3,2,128,128]{5,0,4,3,2,1:T(1,128)S(1)} fusion(f32[4,4,3,2,128,128]{5,4,3,2,1,0:T(8,128)S(1)} %get-tuple-element.65, f32[2,4]{1,0:T(2,128)S(1)} %fusion.36), kind=kOutput, calls=%fused_computation.8 | convolution fusion | flops 18874368 | bytes 7864832 | tf_op jit(solution)/shard_map/ak,kesrij->aesrij/dot_general | solution.py:159
  1257.7 13.9 %fusion = f32[1,4,3,2,128,128]{5,0,4,3,2,1:T(1,128)S(1)} fusion(f32[4,4,3,2,128,128]{5,4,3,2,1,0:T(8,128)S(1)} %bitcast.900, f32[2,4]{1,0:T(2,128)S(1)} %fusion.36), kind=kOutput, calls=%fused_computation.6 | convolution fusion | flops 18874368 | bytes 7864832 | tf_op jit(solution)/shard_map/ak,kesrij->aesrij/dot_general | solution.py:159
  1271.6 1.9 fusion.47
  (359 shorter events, 167.4 us)
Async XLA Ops:
  7.2 903.0 %all-gather.2.cloned.1.call-start = ((), (), s32[]{:S(2)}) async-start(), calls=%async_computation | async-start | bytes 7864320 | tf_op jit(solution)/shard_map/all_gather | solution.py:192
  7.3 60.4 %copy-start.56 = (pred[128,128]{1,0:T(8,128)(4,1)}, pred[128,128]{1,0:T(8,128)(4,1)S(1)}, u32[]{:S(2)}) copy-start(pred[128,128]{1,0:T(8,128)(4,1)S(1)} %iota_compare_fusion.1) | copy-start | bytes 49156
  7.4 388.5 %copy-start.36 = (pred[256,256]{1,0:T(8,128)(4,1)}, pred[256,256]{1,0:T(8,128)(4,1)S(1)}, u32[]{:S(2)}) copy-start(pred[256,256]{1,0:T(8,128)(4,1)S(1)} %iota_compare_fusion) | copy-start | bytes 196612
  16.8 233.7 %copy-start.51 = (f32[128,128]{0,1:T(8,128)}, f32[128,128]{0,1:T(8,128)S(1)}, u32[]{:S(2)}) copy-start(f32[128,128]{0,1:T(8,128)S(1)} %copy.266) | copy-start | bytes 196612
  159.6 87.2 %copy-start.2 = (f32[2,128,128]{2,1,0:T(8,128)S(1)}, f32[2,128,128]{2,1,0:T(8,128)}, u32[]{:S(2)}) copy-start(f32[2,128,128]{2,1,0:T(8,128)} %param.18) | copy-start | bytes 393220
  163.7 83.7 %copy-start.63 = (s32[2,2]{1,0:T(2,128)}, s32[2,2]{1,0:T(2,128)S(1)}, u32[]{:S(2)}) copy-start(s32[2,2]{1,0:T(2,128)S(1)} %get-tuple-element.256) | copy-start | bytes 52
  248.1 8.5 copy-start.52
  251.9 54.4 %copy-start.57 = (pred[128,128]{1,0:T(8,128)(4,1)S(1)}, pred[128,128]{1,0:T(8,128)(4,1)}, u32[]{:S(2)}) copy-start(pred[128,128]{1,0:T(8,128)(4,1)} %copy-done.56) | copy-start | bytes 49156
  255.2 140.9 %copy-start.64 = (s32[2,2]{1,0:T(2,128)S(1)}, s32[2,2]{1,0:T(2,128)}, u32[]{:S(2)}) copy-start(s32[2,2]{1,0:T(2,128)} %copy-done.63) | copy-start | bytes 52
  479.1 11.8 copy-start.50
  489.7 13.0 %copy-start.40 = (bf16[1,4,2,128,128]{4,3,1,2,0:T(8,128)(2,1)S(1)}, bf16[1,4,2,128,128]{4,3,1,2,0:T(8,128)(2,1)}, u32[]{:S(2)}) copy-start(bf16[1,4,2,128,128]{4,3,1,2,0:T(8,128)(2,1)} %get-tuple-element.88) | copy-start | bytes 786436
  492.7 12.7 copy-start.29
  745.6 8.9 copy-start.41
  745.6 8.9 copy-start.47
  754.8 8.8 copy-start.30
  755.5 12.4 copy-start.8
  757.6 26.9 %copy-start.10 = (f32[4,128,128]{1,2,0:T(8,128)}, f32[4,128,128]{1,2,0:T(8,128)S(1)}, u32[]{:S(2)}) copy-start(f32[4,128,128]{1,2,0:T(8,128)S(1)} %convolution_subtract_fusion.24) | copy-start | bytes 786436
  759.8 9.2 copy-start.19
  762.5 9.3 copy-start.18
  763.1 25.7 %copy-start.15 = (f32[4,128,128]{1,2,0:T(8,128)}, f32[4,128,128]{1,2,0:T(8,128)S(1)}, u32[]{:S(2)}) copy-start(f32[4,128,128]{1,2,0:T(8,128)S(1)} %convolution_add_fusion.13) | copy-start | bytes 786436
  768.9 13.7 %copy-start.4 = (f32[4,128,128]{2,1,0:T(8,128)}, f32[4,128,128]{2,1,0:T(8,128)S(1)}, u32[]{:S(2)}) copy-start(f32[4,128,128]{2,1,0:T(8,128)S(1)} %fusion.174) | copy-start | bytes 786436
  773.1 10.6 copy-start.16
  774.2 10.4 copy-start.20
  779.7 9.1 copy-start.24
  783.7 11.5 copy-start.5
  800.3 10.7 copy-start.7
  800.3 11.8 copy-start.13
  800.3 11.8 copy-start.34
  802.3 9.8 copy-start.35
  802.4 13.1 %copy-start.17 = (f32[4,128,128]{2,1,0:T(8,128)S(1)}, f32[4,128,128]{2,1,0:T(8,128)}, u32[]{:S(2)}) copy-start(f32[4,128,128]{2,1,0:T(8,128)} %copy-done.16) | copy-start | bytes 786436
  802.4 14.6 %copy-start.14 = (f32[1,4,128,128]{3,2,1,0:T(8,128)S(1)}, f32[1,4,128,128]{3,2,1,0:T(8,128)}, u32[]{:S(2)}) copy-start(f32[1,4,128,128]{3,2,1,0:T(8,128)} %copy-done.12) | copy-start | bytes 786436
  802.4 17.1 %copy-start.9 = (f32[4,128,128]{1,2,0:T(8,128)S(1)}, f32[4,128,128]{1,2,0:T(8,128)}, u32[]{:S(2)}) copy-start(f32[4,128,128]{1,2,0:T(8,128)} %copy-done.8) | copy-start | bytes 786436
  803.7 11.0 copy-start.21
  807.2 22.9 %copy-start.11 = (f32[4,128,128]{1,2,0:T(8,128)S(1)}, f32[4,128,128]{1,2,0:T(8,128)}, u32[]{:S(2)}) copy-start(f32[4,128,128]{1,2,0:T(8,128)} %copy-done.10) | copy-start | bytes 786436
  816.9 23.0 %copy-start.23 = (f32[1,4,128,128]{3,2,1,0:T(8,128)S(1)}, f32[1,4,128,128]{3,2,1,0:T(8,128)}, u32[]{:S(2)}) copy-start(f32[1,4,128,128]{3,2,1,0:T(8,128)} %copy-done.22) | copy-start | bytes 786436
  830.1 22.6 %copy-start.53 = (bf16[1,4,1,128,128]{3,4,1,2,0:T(8,128)(2,1)S(1)}, bf16[1,4,1,128,128]{3,4,1,2,0:T(8,128)(2,1)}, u32[]{:S(2)}) copy-start(bf16[1,4,1,128,128]{3,4,1,2,0:T(8,128)(2,1)} %convert_bitcast_fusion) | copy-start | bytes 393220
  853.7 62.7 %copy-start.60 = (s32[2]{0:T(128)S(1)}, s32[2]{0:T(128)}, u32[]{:S(2)}) copy-start(s32[2]{0:T(128)} %param.24) | copy-start | bytes 28
  853.7 68.5 %copy-start.61 = (f32[2]{0:T(128)S(1)}, f32[2]{0:T(128)}, u32[]{:S(2)}) copy-start(f32[2]{0:T(128)} %param.23) | copy-start | bytes 28
  853.7 71.2 %copy-start.62 = (f32[2,4]{1,0:T(2,128)S(1)}, f32[2,4]{1,0:T(2,128)}, u32[]{:S(2)}) copy-start(f32[2,4]{1,0:T(2,128)} %param.21) | copy-start | bytes 100
  853.8 71.3 %copy-start.58 = (f32[2,128,128]{2,1,0:T(8,128)S(1)}, f32[2,128,128]{2,1,0:T(8,128)}, u32[]{:S(2)}) copy-start(f32[2,128,128]{2,1,0:T(8,128)} %param.22) | copy-start | bytes 393220
  910.2 137.2 %collective-permute-start = (bf16[4,4,2,3,2,128,128]{6,5,4,3,2,1,0:T(8,128)(2,1)}, bf16[4,4,2,3,2,128,128]{6,5,4,3,2,1,0:T(8,128)(2,1)}, u32[]{:S(2)}, u32[]{:S(2)}) collective-permute-start(bf16[4,4,2,3,2,128,128]{6,5,4,3,2,1,0:T(8,128)(2,1)} %all-gather.2.cloned.1.call-done), channel_id=1, source_target_pairs={{0,1},{1,2},{2,3},{3,4},{4,5},{5,6},{6,7},{7,8},{8,9},{9,10},{10,1... | collective-permute-start | bytes 18874376 | tf_op jit(solution)/shard_map/ppermute | solution.py:15
  915.1 269.9 %collective-permute-start.1 = (bf16[4,4,2,3,2,128,128]{6,5,4,3,2,1,0:T(8,128)(2,1)}, bf16[4,4,2,3,2,128,128]{6,5,4,3,2,1,0:T(8,128)(2,1)}, u32[]{:S(2)}, u32[]{:S(2)}) collective-permute-start(bf16[4,4,2,3,2,128,128]{6,5,4,3,2,1,0:T(8,128)(2,1)} %all-gather.2.cloned.1.call-done), channel_id=1, source_target_pairs={{1,0},{2,1},{3,2},{4,3},{5,4},{6,5},{7,6},{8,7},{9,8},{10,9},{11,1... | collective-permute-start | bytes 18874376 | tf_op jit(solution)/shard_map/ppermute | solution.py:18
  925.1 130.3 %slice-start.2 = ((s8[6291456]{0:T(1024)(128)(4,1)}), s8[4194304]{0:T(1024)(128)(4,1)S(1)}, s32[]{:S(2)}) async-start(s8[6291456]{0:T(1024)(128)(4,1)} %bitcast.901), calls=%async_computation.3 | async-start | bytes 8388608
  925.1 130.2 %slice-start.3 = ((s8[6291456]{0:T(1024)(128)(4,1)}), s8[2097152]{0:T(1024)(128)(4,1)S(1)}, s32[]{:S(2)}) async-start(s8[6291456]{0:T(1024)(128)(4,1)} %bitcast.901), calls=%async_computation.4 | async-start | bytes 4194304
  1211.2 19.0 %copy-start.3 = (f32[4,4,3,2,128,128]{5,4,3,2,1,0:T(8,128)S(1)}, f32[4,4,3,2,128,128]{5,4,3,2,1,0:T(8,128)}, u32[]{:S(2)}) copy-start(f32[4,4,3,2,128,128]{5,4,3,2,1,0:T(8,128)} %get-tuple-element.66) | copy-start | bytes 18874372
  1230.2 27.5 %slice-start = ((s8[6291456]{0:T(1024)(128)(4,1)}), s8[4194304]{0:T(1024)(128)(4,1)S(1)}, s32[]{:S(2)}) async-start(s8[6291456]{0:T(1024)(128)(4,1)} %bitcast.899), calls=%async_computation.1 | async-start | bytes 8388608
  1244.1 13.6 %slice-start.1 = ((s8[6291456]{0:T(1024)(128)(4,1)}), s8[2097152]{0:T(1024)(128)(4,1)S(1)}, s32[]{:S(2)}) async-start(s8[6291456]{0:T(1024)(128)(4,1)} %bitcast.899), calls=%async_computation.2 | async-start | bytes 4194304
  1257.7 15.8 %copy-start.1 = (f32[3,128,128]{2,1,0:T(8,128)S(1)}, f32[3,128,128]{2,1,0:T(8,128)}, u32[]{:S(2)}) copy-start(f32[3,128,128]{2,1,0:T(8,128)} %param.16) | copy-start | bytes 589828
  (24 other events, 91.1 us)
Sparse Core Ops, SparseCore 0:
  856.1 54.0 all-gather.1
where the time goes:
time: 1290 us; the launch traced here: 1280 us
  other arithmetic  684 us (53%)
  waiting for transfers between devices  302 us (23%)
  matrix products  181 us (14%)
  local copies, waits for them, and re-layouts  83.6 us (6%)
  between operations  22.8 us (2%)
    another operation x26, other arithmetic, invert_pair(): factor = jnp.linalg.cholesky(normal)  407 us
    another operation x8, other arithmetic, invert_pair(): solved = jax.scipy.linalg.cho_solve((factor, True), transposed)  241 us
    ppermute x1, waiting for transfers between devices, padded(): lax.ppermute(lax.slice_in_dim(block, 0, width, axis=dim), axis, backward)  126 us
    ppermute x1, waiting for transfers between devices, padded(): lax.ppermute(lax.slice_in_dim(block, block.shape[dim] - width, None, axis...  122 us
    dot_general x95, matrix products, matmul_high(): jnp.matmul(left_matrix, right_matrix, precision=lax.Precision.HIGHEST)  89.9 us
    all_gather x1, waiting for transfers between devices, on_device(): everyone = lax.all_gather(blocks, 'kz', axis=0, tiled=True)  54.2 us
    dot_general x2, matrix products, mixed_sums(): jnp.einsum('ak,kesrij->aesrij', weights[mode_index], less_term, precision...  32.8 us
    dot_general x2, matrix products, mixed_sums(): jnp.einsum('ak,kesrij->aesrij', weights[mode_index], great_term, precisio...  27.5 us
  transfers between devices with their start and end apart: 3, of which 3 were waited for; matrix products, arithmetic and copies ran while one was open for 1% of the time, Pallas kernels for 0%

commit v1 on v0

--- a/solution.py
+++ b/solution.py
@@ -189,7 +189,9 @@
     blocks = green_blocks(sigma_less, sigma_great, hamilton, slab_coupling, energies)
     table_rows = lax.dynamic_slice_in_dim(kz_table, momenta_start, momenta_local, 0)
     weights = momentum_weights(table_rows, mode_weight, momenta_total)
-    everyone = lax.all_gather(blocks, "kz", axis=0, tiled=True)
+    everyone = jnp.concatenate(
+        lax.all_to_all(jnp.stack([blocks] * lax.axis_size("kz")), "kz", 0, 0), axis=0
+    )
     extended = padded(everyone, (("en", 1),), OFFMAX)
     less_total, great_total = mixed_sums(
         extended, weights, form_factor, occupation, energy_offset, energy_local, OFFMAX

time: 1290 us -> 1320 us (1.023)
  blocking collectives: 0 us -> 76.9 us
  waiting for transfers between devices: 302 us -> 259 us
  other arithmetic: 684 us -> 710 us
  local copies, waits for them, and re-layouts: 83.6 us -> 67.5 us
  between operations: 22.8 us -> 9.37 us
    all_to_all x0 -> x1, blocking collectives: none -> 76.9 us  [on_device(): lax.all_to_all(jnp.stack([blocks] * lax.axis_size('kz')), 'kz', 0, 0)]
    all_gather x1 -> x0, waiting for transfers between devices: 54.2 us -> none  [on_device(): everyone = lax.all_gather(blocks, 'kz', axis=0, tiled=True)]
    concatenate x0 -> x1, other arithmetic: none -> 15 us  [padded(): block = jnp.concatenate([low, block, high], axis=dim)]
  transfers between devices with their start and end apart: 3 -> 2, of which waited for: 3 -> 2; matrix products, arithmetic and copies ran while one was open for 1% -> 0% of each run, Pallas kernels for 0% -> 0%
where the time goes in v1:
time: 1320 us
  other arithmetic  710 us (54%)
  waiting for transfers between devices  259 us (20%)
  matrix products  188 us (14%)
  blocking collectives  76.9 us (6%)
  local copies, waits for them, and re-layouts  67.5 us (5%)
    another operation x26, other arithmetic, invert_pair(): factor = jnp.linalg.cholesky(normal)  411 us
    another operation x8, other arithmetic, invert_pair(): solved = jax.scipy.linalg.cho_solve((factor, True), transposed)  243 us
    ppermute x1, waiting for transfers between devices, padded(): lax.ppermute(lax.slice_in_dim(block, 0, width, axis=dim), axis, backward)  137 us
    ppermute x1, waiting for transfers between devices, padded(): lax.ppermute(lax.slice_in_dim(block, block.shape[dim] - width, None, axis...  121 us
    dot_general x95, matrix products, matmul_high(): jnp.matmul(left_matrix, right_matrix, precision=lax.Precision.HIGHEST)  96.6 us
    all_to_all x1, blocking collectives, on_device(): lax.all_to_all(jnp.stack([blocks] * lax.axis_size('kz')), 'kz', 0, 0)  76.9 us
    dot_general x2, matrix products, mixed_sums(): jnp.einsum('ak,kesrij->aesrij', weights[mode_index], less_term, precision...  32.8 us
    dot_general x2, matrix products, mixed_sums(): jnp.einsum('ak,kesrij->aesrij', weights[mode_index], great_term, precisio...  27.5 us
  transfers between devices with their start and end apart: 2, of which 2 were waited for; matrix products, arithmetic and copies ran while one was open for 0% of the time, Pallas kernels for 0%

profile of v1, /device:TPU:1, one launch (start us, length us, event | category | flops | bytes accessed | tf_op | source)
XLA Modules:
  0.0 1316.6 jit_solution(13449929627954015853)
XLA Ops:
  1.9 2.0 fusion.356
  12.8 47.1 %custom-call.23 = f32[1,4,128,128]{3,2,1,0:T(8,128)S(1)} custom-call(f32[1,4,128,128]{3,2,1,0:T(8,128)S(1)} %cholesky.281), custom_call_target="Cholesky" | custom-call | tf_op jit(solution)/shard_map/jit(cholesky)/cholesky | solution.py:60
  60.0 39.3 %custom-call.24 = f32[1,4,1,128,128]{3,4,2,1,0:T(8,128)S(1)} custom-call(f32[1,4,1,128,128]{4,3,2,1,0:T(8,128)S(1)} %select_bitcast_fusion.2), custom_call_target="InvertDiagBlocksLowerTriangular" | custom-call | tf_op jit(solution)/shard_map/jit(cholesky)/cholesky | solution.py:60
  102.4 46.9 %custom-call.25 = f32[1,4,128,128]{3,2,1,0:T(8,128)S(1)} custom-call(f32[1,4,128,128]{3,2,1,0:T(8,128)S(1)} %fusion.25), custom_call_target="Cholesky" | custom-call | tf_op jit(solution)/shard_map/jit(cholesky)/cholesky | solution.py:60
  149.9 4.1 while.6
  154.0 78.8 %custom-call.26 = f32[4,2,128,128]{2,3,1,0:T(8,128)S(1)} custom-call(f32[4,2,128,128]{3,2,1,0:T(8,128)S(1)} %bitcast.916), custom_call_target="InvertDiagBlocksLowerTriangular" | custom-call | tf_op jit(solution)/shard_map/jit(_cho_solve)/vmap()/triangular_solve | solution.py:61
  243.4 2.2 fusion.42
  246.6 2.5 copy.272
  251.9 47.3 %custom-call.27 = f32[1,4,128,128]{3,2,1,0:T(8,128)S(1)} custom-call(f32[1,4,128,128]{3,2,1,0:T(8,128)S(1)} %cholesky.284), custom_call_target="Cholesky" | custom-call | tf_op jit(solution)/shard_map/jit(cholesky)/cholesky | solution.py:60
  301.7 40.7 %custom-call.28 = f32[1,4,1,128,128]{3,4,2,1,0:T(8,128)} custom-call(f32[1,4,1,128,128]{4,3,2,1,0:T(8,128)} %select_bitcast_fusion.1), custom_call_target="InvertDiagBlocksLowerTriangular" | custom-call | tf_op jit(solution)/shard_map/jit(cholesky)/cholesky | solution.py:60
  343.8 2.3 fusion.26
  346.2 48.3 %custom-call.29 = f32[1,4,128,128]{3,2,1,0:T(8,128)} custom-call(f32[1,4,128,128]{3,2,1,0:T(8,128)} %fusion.26), custom_call_target="Cholesky" | custom-call | tf_op jit(solution)/shard_map/jit(cholesky)/cholesky | solution.py:60
  398.9 5.2 while.7
  399.5 2.0 bitcast_dynamic-update-slice_fusion.10
  402.1 2.0 bitcast_dynamic-update-slice_fusion.10
  404.1 80.2 %custom-call.30 = f32[4,2,128,128]{2,3,1,0:T(8,128)} custom-call(f32[4,2,128,128]{3,2,1,0:T(8,128)} %bitcast.917), custom_call_target="InvertDiagBlocksLowerTriangular" | custom-call | tf_op jit(solution)/shard_map/jit(_cho_solve)/vmap()/triangular_solve | solution.py:61
  502.9 3.2 fusion.40
  506.1 2.1 fusion.48
  518.5 47.3 %custom-call.31 = f32[1,4,128,128]{3,2,1,0:T(8,128)S(1)} custom-call(f32[1,4,128,128]{3,2,1,0:T(8,128)S(1)} %cholesky.287), custom_call_target="Cholesky" | custom-call | tf_op jit(solution)/shard_map/jit(cholesky)/cholesky | solution.py:60
  568.3 40.7 %custom-call.32 = f32[1,4,1,128,128]{3,4,2,1,0:T(8,128)} custom-call(f32[1,4,1,128,128]{4,3,2,1,0:T(8,128)} %select_bitcast_fusion), custom_call_target="InvertDiagBlocksLowerTriangular" | custom-call | tf_op jit(solution)/shard_map/jit(cholesky)/cholesky | solution.py:60
  610.4 2.3 fusion.27
  612.8 48.3 %custom-call.33 = f32[1,4,128,128]{3,2,1,0:T(8,128)} custom-call(f32[1,4,128,128]{3,2,1,0:T(8,128)} %fusion.27), custom_call_target="Cholesky" | custom-call | tf_op jit(solution)/shard_map/jit(cholesky)/cholesky | solution.py:60
  665.4 5.4 while.8
  666.0 2.1 bitcast_dynamic-update-slice_fusion.11
  668.7 2.1 bitcast_dynamic-update-slice_fusion.11
  670.8 80.2 %custom-call.34 = f32[4,2,128,128]{2,3,1,0:T(8,128)} custom-call(f32[4,2,128,128]{3,2,1,0:T(8,128)} %bitcast.915), custom_call_target="InvertDiagBlocksLowerTriangular" | custom-call | tf_op jit(solution)/shard_map/jit(_cho_solve)/vmap()/triangular_solve | solution.py:61
  799.9 2.0 fusion.32
  802.6 2.1 fusion.97
  804.6 2.2 fusion.17
  808.6 2.0 fusion.33
  810.6 2.4 fusion.93
  817.9 2.4 fusion.370
  820.3 2.1 fusion.162
  833.0 2.3 convolution_subtract_fusion.7
  837.1 2.1 fusion.30
  846.8 2.2 fusion.31
  860.8 2.1 convert_bitcast_fusion.5
  862.9 2.0 convert_bitcast_fusion.4
  870.3 76.9 %all_to_all.5 = bf16[4,1,4,2,3,2,128,128]{7,6,5,4,3,2,1,0:T(8,128)(2,1)} all-to-all(bf16[4,1,4,2,3,2,128,128]{7,6,5,4,3,2,1,0:T(8,128)(2,1)S(1)} %stack.149), channel_id=1, replica_groups=mesh['kz'=4,'en'=32] {'kz'}, dimensions={0} | all-to-all | bytes 12582912 | tf_op jit(solution)/shard_map/all_to_all | solution.py:193
  947.2 5.2 collective-permute-start
  962.4 121.3 %collective-permute-done = bf16[4,4,2,3,2,128,128]{6,5,4,3,2,1,0:T(8,128)(2,1)} collective-permute-done((bf16[4,4,2,3,2,128,128]{6,5,4,3,2,1,0:T(8,128)(2,1)}, bf16[4,4,2,3,2,128,128]{6,5,4,3,2,1,0:T(8,128)(2,1)}, u32[]{:S(2)}, u32[]{:S(2)}) %collective-permute-start) | collective-permute-done | bytes 6291488 | tf_op jit(solution)/shard_map/ppermute | solution.py:15
  1083.7 137.4 %collective-permute-done.1 = bf16[4,4,2,3,2,128,128]{6,5,4,3,2,1,0:T(8,128)(2,1)} collective-permute-done((bf16[4,4,2,3,2,128,128]{6,5,4,3,2,1,0:T(8,128)(2,1)}, bf16[4,4,2,3,2,128,128]{6,5,4,3,2,1,0:T(8,128)(2,1)}, u32[]{:S(2)}, u32[]{:S(2)}) %collective-permute-start.1) | collective-permute-done | bytes 6291488 | tf_op jit(solution)/shard_map/ppermute | solution.py:18
  1221.2 15.0 %pad_maximum_fusion = bf16[4,12,2,3,2,128,128]{6,5,4,3,2,1,0:T(8,128)(2,1)} fusion(bf16[4,4,2,3,2,128,128]{6,5,4,3,2,1,0:T(8,128)(2,1)} %collective-permute-done.1, bf16[4,4,2,3,2,128,128]{6,5,4,3,2,1,0:T(8,128)(2,1)} %bitcast.201, bf16[4,4,2,3,2,128,128]{6,5,4,3,2,1,0:T(8,128)(2,1)} %collective-permute-done), kind=kLoop, calls=%fused_computation.6 | loop fusion | flops 18874368 | bytes 37748736 | tf_op jit(solution)/shard_map/concatenate | solution.py:19
  1236.2 17.9 %add_bitcast_fusion.1 = (f32[4,4,3,2,128,128]{5,4,3,2,1,0:T(8,128)}, f32[4,4,3,2,128,128]{5,4,3,2,1,0:T(8,128)}, f32[4,4,3,2,128,128]{5,4,3,2,1,0:T(8,128)S(1)}, f32[4,4,3,2,128,128]{5,4,3,2,1,0:T(8,128)}) fusion(bf16[4,12,2,3,2,128,128]{6,5,4,3,2,1,0:T(8,128)(2,1)} %pad_maximum_fusion, s32[]{:T(128)S(6)} %select_n.19, s32[]{:T(128)S(6)} %add.377, ...), kind=kLoop, calls=%fused_computation.16 | loop fusion | flops 31457280 | bytes 50331684 | tf_op jit(solution)/shard_map/add | solution.py:153
  1254.2 19.0 %fusion.6 = f32[1,4,3,2,128,128]{5,0,4,3,2,1:T(1,128)S(1)} fusion(f32[4,4,3,2,128,128]{5,4,3,2,1,0:T(8,128)} %get-tuple-element.68, f32[2,4]{1,0:T(2,128)S(1)} %fusion.36), kind=kOutput, calls=%fused_computation.13 | convolution fusion | flops 18874368 | bytes 7864832 | tf_op jit(solution)/shard_map/ak,kesrij->aesrij/dot_general | solution.py:156
  1273.2 13.8 %fusion.4 = f32[1,4,3,2,128,128]{5,0,4,3,2,1:T(1,128)S(1)} fusion(f32[4,4,3,2,128,128]{5,4,3,2,1,0:T(8,128)S(1)} %copy-done.3, f32[2,4]{1,0:T(2,128)S(1)} %fusion.36), kind=kOutput, calls=%fused_computation.11 | convolution fusion | flops 18874368 | bytes 7864832 | tf_op jit(solution)/shard_map/ak,kesrij->aesrij/dot_general | solution.py:156
  1287.0 13.6 %fusion.2 = f32[1,4,3,2,128,128]{5,0,4,3,2,1:T(1,128)S(1)} fusion(f32[4,4,3,2,128,128]{5,4,3,2,1,0:T(8,128)S(1)} %bitcast.901, f32[2,4]{1,0:T(2,128)S(1)} %fusion.36), kind=kOutput, calls=%fused_computation.9 | convolution fusion | flops 18874368 | bytes 7864832 | tf_op jit(solution)/shard_map/ak,kesrij->aesrij/dot_general | solution.py:159
  1300.7 13.8 %fusion = f32[1,4,3,2,128,128]{5,0,4,3,2,1:T(1,128)S(1)} fusion(f32[4,4,3,2,128,128]{5,4,3,2,1,0:T(8,128)S(1)} %get-tuple-element.67, f32[2,4]{1,0:T(2,128)S(1)} %fusion.36), kind=kOutput, calls=%fused_computation.7 | convolution fusion | flops 18874368 | bytes 7864832 | tf_op jit(solution)/shard_map/ak,kesrij->aesrij/dot_general | solution.py:159
  (347 shorter events, 177.0 us)
Async XLA Ops:
  9.2 50.7 %copy-start.52 = (pred[128,128]{1,0:T(8,128)(4,1)S(1)}, pred[128,128]{1,0:T(8,128)(4,1)}, u32[]{:S(2)}) copy-start(pred[128,128]{1,0:T(8,128)(4,1)} %iota_compare_fusion.1) | copy-start | bytes 49156
  11.3 138.5 %copy-start.62 = (s32[2]{0:T(128)S(1)}, s32[2]{0:T(128)}, u32[]{:S(2)}) copy-start(s32[2]{0:T(128)} %iota_multiply_fusion) | copy-start | bytes 28
  149.9 87.2 %copy-start.2 = (f32[2,128,128]{2,1,0:T(8,128)S(1)}, f32[2,128,128]{2,1,0:T(8,128)}, u32[]{:S(2)}) copy-start(f32[2,128,128]{2,1,0:T(8,128)} %param.18) | copy-start | bytes 393220
  154.0 83.7 %copy-start.60 = (s32[2,2]{1,0:T(2,128)}, s32[2,2]{1,0:T(2,128)S(1)}, u32[]{:S(2)}) copy-start(s32[2,2]{1,0:T(2,128)S(1)} %get-tuple-element.250) | copy-start | bytes 52
  240.8 10.0 copy-start.24
  242.3 57.6 %copy-start.53 = (pred[128,128]{1,0:T(8,128)(4,1)S(1)}, pred[128,128]{1,0:T(8,128)(4,1)}, u32[]{:S(2)}) copy-start(pred[128,128]{1,0:T(8,128)(4,1)} %iota_compare_fusion.1) | copy-start | bytes 49156
  246.6 152.3 %copy-start.61 = (s32[2,2]{1,0:T(2,128)S(1)}, s32[2,2]{1,0:T(2,128)}, u32[]{:S(2)}) copy-start(s32[2,2]{1,0:T(2,128)} %copy-done.60) | copy-start | bytes 52
  488.2 13.3 %copy-start.56 = (f32[4]{0:T(128)S(1)}, f32[4]{0:T(128)}, u32[]{:S(2)}) copy-start(f32[4]{0:T(128)} %copy-done.55) | copy-start | bytes 52
  493.7 16.6 %copy-start.36 = (bf16[1,4,2,128,128]{4,3,1,2,0:T(8,128)(2,1)S(1)}, bf16[1,4,2,128,128]{4,3,1,2,0:T(8,128)(2,1)}, u32[]{:S(2)}) copy-start(bf16[1,4,2,128,128]{4,3,1,2,0:T(8,128)(2,1)} %get-tuple-element.88) | copy-start | bytes 786436
  497.7 15.5 %copy-start.26 = (f32[1,4,2,128,128]{3,4,1,2,0:T(8,128)}, f32[1,4,2,128,128]{3,4,1,2,0:T(8,128)S(1)}, u32[]{:S(2)}) copy-start(f32[1,4,2,128,128]{3,4,1,2,0:T(8,128)S(1)} %get-tuple-element.113) | copy-start | bytes 1572868
  751.0 7.4 copy-start.43
  751.0 10.8 copy-start.37
  751.0 10.8 copy-start.45
  752.9 9.3 copy-start.48
  754.6 8.7 copy-start.25
  756.2 8.1 copy-start.47
  762.1 8.8 copy-start.27
  762.8 7.7 copy-start.7
  765.0 26.9 %copy-start.9 = (f32[4,128,128]{1,2,0:T(8,128)}, f32[4,128,128]{1,2,0:T(8,128)S(1)}, u32[]{:S(2)}) copy-start(f32[4,128,128]{1,2,0:T(8,128)S(1)} %convolution_subtract_fusion.24) | copy-start | bytes 786436
  767.1 9.2 copy-start.16
  769.8 9.2 copy-start.15
  770.5 24.3 %copy-start.13 = (f32[4,128,128]{1,2,0:T(8,128)}, f32[4,128,128]{1,2,0:T(8,128)S(1)}, u32[]{:S(2)}) copy-start(f32[4,128,128]{1,2,0:T(8,128)S(1)} %convolution_add_fusion.13) | copy-start | bytes 786436
  770.9 9.5 copy-start.4
  776.3 13.7 %copy-start.5 = (f32[4,128,128]{2,1,0:T(8,128)}, f32[4,128,128]{2,1,0:T(8,128)S(1)}, u32[]{:S(2)}) copy-start(f32[4,128,128]{2,1,0:T(8,128)S(1)} %fusion.174) | copy-start | bytes 786436
  780.4 10.6 copy-start.14
  781.5 10.3 copy-start.17
  787.1 9.1 copy-start.20
  788.7 7.5 copy-start.22
  789.6 6.6 copy-start.19
  808.6 13.8 %copy-start.31 = (f32[1,4,128,128]{3,2,1,0:T(8,128)S(1)}, f32[1,4,128,128]{3,2,1,0:T(8,128)}, u32[]{:S(2)}) copy-start(f32[1,4,128,128]{3,2,1,0:T(8,128)} %copy-done.30) | copy-start | bytes 786436
  810.6 22.3 %copy-start.8 = (f32[4,128,128]{1,2,0:T(8,128)S(1)}, f32[4,128,128]{1,2,0:T(8,128)}, u32[]{:S(2)}) copy-start(f32[4,128,128]{1,2,0:T(8,128)} %copy-done.7) | copy-start | bytes 786436
  814.8 26.2 %copy-start.21 = (f32[4,128,128]{2,1,0:T(8,128)S(1)}, f32[4,128,128]{2,1,0:T(8,128)}, u32[]{:S(2)}) copy-start(f32[4,128,128]{2,1,0:T(8,128)} %copy-done.20) | copy-start | bytes 786436
  816.6 27.0 %copy-start.10 = (f32[4,128,128]{1,2,0:T(8,128)S(1)}, f32[4,128,128]{1,2,0:T(8,128)}, u32[]{:S(2)}) copy-start(f32[4,128,128]{1,2,0:T(8,128)} %copy-done.9) | copy-start | bytes 786436
  828.5 28.4 %copy-start.12 = (f32[1,4,128,128]{3,2,1,0:T(8,128)S(1)}, f32[1,4,128,128]{3,2,1,0:T(8,128)}, u32[]{:S(2)}) copy-start(f32[1,4,128,128]{3,2,1,0:T(8,128)} %copy-done.11) | copy-start | bytes 786436
  843.5 22.5 %copy-start.50 = (bf16[1,4,1,128,128]{3,4,1,2,0:T(8,128)(2,1)S(1)}, bf16[1,4,1,128,128]{3,4,1,2,0:T(8,128)(2,1)}, u32[]{:S(2)}) copy-start(bf16[1,4,1,128,128]{3,4,1,2,0:T(8,128)(2,1)} %convert_bitcast_fusion) | copy-start | bytes 393220
  846.8 20.2 %copy-start.18 = (f32[4,128,128]{1,2,0:T(8,128)S(1)}, f32[4,128,128]{1,2,0:T(8,128)}, u32[]{:S(2)}) copy-start(f32[4,128,128]{1,2,0:T(8,128)} %copy-done.17) | copy-start | bytes 786436
  860.8 6.2 copy-start.51
  860.8 6.2 copy-start.49
  870.2 83.5 %copy-start.57 = (s32[2]{0:T(128)S(1)}, s32[2]{0:T(128)}, u32[]{:S(2)}) copy-start(s32[2]{0:T(128)} %param.24) | copy-start | bytes 28
  870.2 89.3 %copy-start.58 = (f32[2]{0:T(128)S(1)}, f32[2]{0:T(128)}, u32[]{:S(2)}) copy-start(f32[2]{0:T(128)} %param.23) | copy-start | bytes 28
  870.2 92.0 %copy-start.59 = (f32[2,4]{1,0:T(2,128)S(1)}, f32[2,4]{1,0:T(2,128)}, u32[]{:S(2)}) copy-start(f32[2,4]{1,0:T(2,128)} %param.21) | copy-start | bytes 100
  870.2 92.2 %copy-start.54 = (f32[2,128,128]{2,1,0:T(8,128)S(1)}, f32[2,128,128]{2,1,0:T(8,128)}, u32[]{:S(2)}) copy-start(f32[2,128,128]{2,1,0:T(8,128)} %param.22) | copy-start | bytes 393220
  947.2 136.6 %collective-permute-start = (bf16[4,4,2,3,2,128,128]{6,5,4,3,2,1,0:T(8,128)(2,1)}, bf16[4,4,2,3,2,128,128]{6,5,4,3,2,1,0:T(8,128)(2,1)}, u32[]{:S(2)}, u32[]{:S(2)}) collective-permute-start(bf16[4,4,2,3,2,128,128]{6,5,4,3,2,1,0:T(8,128)(2,1)} %bitcast.201), channel_id=1, source_target_pairs={{0,1},{1,2},{2,3},{3,4},{4,5},{5,6},{6,7},{7,8},{8,9},{9,10},{10,1... | collective-permute-start | bytes 18874376 | tf_op jit(solution)/shard_map/ppermute | solution.py:15
  952.4 268.8 %collective-permute-start.1 = (bf16[4,4,2,3,2,128,128]{6,5,4,3,2,1,0:T(8,128)(2,1)}, bf16[4,4,2,3,2,128,128]{6,5,4,3,2,1,0:T(8,128)(2,1)}, u32[]{:S(2)}, u32[]{:S(2)}) collective-permute-start(bf16[4,4,2,3,2,128,128]{6,5,4,3,2,1,0:T(8,128)(2,1)} %bitcast.201), channel_id=1, source_target_pairs={{1,0},{2,1},{3,2},{4,3},{5,4},{6,5},{7,6},{8,7},{9,8},{10,9},{11,1... | collective-permute-start | bytes 18874376 | tf_op jit(solution)/shard_map/ppermute | solution.py:18
  1254.2 19.0 %copy-start.3 = (f32[4,4,3,2,128,128]{5,4,3,2,1,0:T(8,128)S(1)}, f32[4,4,3,2,128,128]{5,4,3,2,1,0:T(8,128)}, u32[]{:S(2)}) copy-start(f32[4,4,3,2,128,128]{5,4,3,2,1,0:T(8,128)} %get-tuple-element.66) | copy-start | bytes 18874372
  1254.2 32.8 %slice-start = ((s8[6291456]{0:T(1024)(128)(4,1)}), s8[4194304]{0:T(1024)(128)(4,1)S(1)}, s32[]{:S(2)}) async-start(s8[6291456]{0:T(1024)(128)(4,1)} %bitcast.900), calls=%async_computation.1 | async-start | bytes 8388608
  1273.2 13.9 %slice-start.1 = ((s8[6291456]{0:T(1024)(128)(4,1)}), s8[2097152]{0:T(1024)(128)(4,1)S(1)}, s32[]{:S(2)}) async-start(s8[6291456]{0:T(1024)(128)(4,1)} %bitcast.900), calls=%async_computation.2 | async-start | bytes 4194304
  1300.7 15.7 %copy-start.1 = (f32[3,128,128]{2,1,0:T(8,128)S(1)}, f32[3,128,128]{2,1,0:T(8,128)}, u32[]{:S(2)}) copy-start(f32[3,128,128]{2,1,0:T(8,128)} %param.16) | copy-start | bytes 589828
  (19 other events, 42.8 us)
